TPU v7x, 128 devices: a whole 4x4x4 slice. The times are simulated.
128 devices in a mesh: epoch: 8 (over z, y_hi), row: 16 (over y_lo, x, core).
Axes of the slice: x: 4, y: 4 (y_hi: 2, y_lo: 2; y = y_hi * 2 + y_lo), z: 4, core: 2. Of those that a mesh axis runs over, the one named last changes fastest.
Arguments:
- field: bfloat16 [1024, 512, 512], P('epoch', 'row'), may hold values from -6 to 6
- factor: bfloat16 [1024, 1024], P('epoch'), may hold values from -0.1875 to 0.1875
- kappa: float32 [512, 512], P('row'), may hold values from 0.05 to 1
Outputs:
- product: float32 [1024, 512, 512], P('epoch', 'row')
All inputs are finite; a program needn't handle non-finite values.
Results may differ from a plain program's by a relative error of at most 0.0004.
Values may be sent and summed in bfloat16 or wider, within the bound.
No kernel may reach another device: no remote copies, remote signals or barrier semaphores. Data moves between devices by JAX's collectives and lax.ppermute only.
A program may use at most 192 MiB of HBM per device.

v0:
```python
import jax
import jax.numpy as jnp
from jax import lax
from jax.sharding import PartitionSpec as P


def with_halo(x, sides, width):
    for axis, dim in sides:
        size, length = (lax.axis_size(axis), x.shape[dim])
        up = [(i, (i + 1) % size) for i in range(size - 1)]
        down = [(j, i) for i, j in up]
        last = lax.slice_in_dim(x, length - width, length, axis=dim)
        first = lax.slice_in_dim(x, 0, width, axis=dim)
        before = lax.ppermute(last, axis, up)
        after = lax.ppermute(first, axis, down)
        x = jnp.concatenate([before, x, after], axis=dim)
    return x


def stencil(padded, kappa):
    center = padded[:, 1:-1, :]
    sides = jnp.pad(center, ((0, 0), (0, 0), (1, 1)))
    upper = padded[:, :-2, :]
    below = padded[:, 2:, :]
    return (kappa + 4.0) * center - (upper + below + sides[:, :, :-2] + sides[:, :, 2:])


def single_rim(values):
    return with_halo(values, (("row", 1),), 1)


def body(field, factor, kappa):
    epochs = field.shape[0]
    slab = field.shape[1]
    width = field.shape[2]
    count = lax.axis_size("epoch")
    order = epochs * count
    global_rows = lax.axis_index("epoch") * epochs + lax.broadcasted_iota(
        jnp.int32, (epochs, order), 0
    )
    global_cols = lax.broadcasted_iota(jnp.int32, (epochs, order), 1)
    lower = jnp.where(global_cols <= global_rows, factor, jnp.zeros_like(factor))
    piece = lax.all_gather(field, "epoch", axis=0, tiled=True)
    many = piece.shape[0]
    timed = jnp.dot(
        lower, piece.reshape(many, slab * width), preferred_element_type=jnp.float32
    ).reshape(epochs, slab, width)
    first = stencil(single_rim(timed), kappa)
    return stencil(single_rim(first), kappa)


def solution(mesh):
    in_specs = (P("epoch", "row", None), P("epoch", None), P("row", None))
    out_specs = P("epoch", "row", None)
    return jax.shard_map(body, mesh=mesh, in_specs=in_specs, out_specs=out_specs, check_vma=False)
```

profile of v0, /device:TPU:7, one launch (start us, length us, event | category | flops | bytes accessed | tf_op | source)
XLA Modules:
  0.0 493.1 jit_solution(14374441201835860905)
XLA Ops:
  6.5 0.0 all-gather.2.cloned.1.call-start
  6.5 0.7 all-gather.2.cloned.1.call-update
  7.3 0.0 copy-start
  7.3 338.7 %all-gather.2.cloned.1.call-done = bf16[1024,32,512]{2,1,0:T(8,128)(2,1)} async-done(((bf16[128,32,512]{2,1,0:T(8,128)(2,1)}), bf16[1024,32,512]{2,1,0:T(8,128)(2,1)}) %all-gather.2.cloned.1.call-update) | async-done | bytes 33554448 | tf_op jit(solution)/shard_map/all_gather | solution.py:43
  345.9 45.1 %copy.8 = bf16[1024,32,512]{0,2,1:T(8,128)(2,1)} copy(bf16[1024,32,512]{2,1,0:T(8,128)(2,1)} %all-gather.2.cloned.1.call-done) | data formatting | bytes 67108864 | tf_op jit(solution)/shard_map/reshape | solution.py:46
  391.1 0.0 copy-done
  391.1 0.0 copy-start.1
  391.1 18.8 %fusion = f32[128,32,512]{2,0,1:T(8,128)} fusion(bf16[1024,32,512]{0,2,1:T(8,128)(2,1)} %copy.8, bf16[128,1024]{1,0:T(8,128)(2,1)S(1)} %copy-done, s32[128]{0:T(128)S(1)} %iota_add_fusion), kind=kOutput, calls=%fused_computation | convolution fusion | flops 4295229440 | bytes 42205696 | tf_op jit(solution)/shard_map/dot_general | solution.py:45
  409.9 1.1 fusion.17
  411.0 3.2 collective-permute-start
  414.1 1.9 collective-permute-start.1
  416.1 0.0 copy-done.1
  416.1 1.3 collective-permute-done
  417.4 6.5 %collective-permute-done.1 = f32[128,1,512]{2,0,1:T(8,128)S(1)} collective-permute-done((f32[128,1,512]{2,0,1:T(8,128)S(1)}, f32[128,1,512]{2,0,1:T(8,128)S(1)}, u32[]{:S(2)}, u32[]{:S(2)}) %collective-permute-start.1) | collective-permute-done | bytes 262176 | tf_op jit(solution)/shard_map/ppermute | solution.py:15
  423.9 18.9 %fusion.4 = f32[128,32,512]{2,0,1:T(8,128)} fusion(f32[128,32,512]{2,0,1:T(8,128)} %fusion, f32[128,1,512]{2,0,1:T(8,128)S(1)} %collective-permute-done.1, f32[128,1,512]{2,0,1:T(8,128)S(1)} %collective-permute-done, f32[32,512]{1,0:T(8,128)S(1)} %broadcast_add_fusion), kind=kLoop, calls=%fused_computation.8 | loop fusion | flops 14680064 | bytes 17367040 | tf_op jit(solution)/shard_map/sub | solution.py:25
  442.9 1.1 fusion.16
  443.9 1.9 collective-permute-start.2
  445.9 2.6 collective-permute-start.3
  448.5 0.7 collective-permute-done.2
  449.2 6.5 %collective-permute-done.3 = f32[128,1,512]{2,0,1:T(8,128)S(1)} collective-permute-done((f32[128,1,512]{2,0,1:T(8,128)S(1)}, f32[128,1,512]{2,0,1:T(8,128)S(1)}, u32[]{:S(2)}, u32[]{:S(2)}) %collective-permute-start.3) | collective-permute-done | bytes 262176 | tf_op jit(solution)/shard_map/ppermute | solution.py:15
  455.7 18.9 %fusion.7 = f32[128,32,512]{2,0,1:T(8,128)} fusion(f32[128,32,512]{2,0,1:T(8,128)} %fusion.4, f32[128,1,512]{2,0,1:T(8,128)S(1)} %collective-permute-done.3, f32[128,1,512]{2,0,1:T(8,128)S(1)} %collective-permute-done.2, f32[32,512]{1,0:T(8,128)S(1)} %broadcast_add_fusion), kind=kLoop, calls=%fused_computation.11 | loop fusion | flops 14680064 | bytes 17367040 | tf_op jit(solution)/shard_map/sub | solution.py:25
  474.6 11.6 %copy.7 = f32[128,32,512]{2,1,0:T(8,128)} copy(f32[128,32,512]{2,0,1:T(8,128)} %fusion.7) | data formatting | bytes 16777216 | tf_op jit(solution)/shard_map/sub | solution.py:25
  (2 shorter events, 0.0 us)
Async XLA Ops:
  6.5 339.4 %all-gather.2.cloned.1.call-start = ((), (), s32[]{:S(2)}) async-start(), calls=%async_computation | async-start | bytes 37748736 | tf_op jit(solution)/shard_map/all_gather | solution.py:43
  7.3 383.8 %copy-start = (bf16[128,1024]{1,0:T(8,128)(2,1)S(1)}, bf16[128,1024]{1,0:T(8,128)(2,1)}, u32[]{:S(2)}) copy-start(bf16[128,1024]{1,0:T(8,128)(2,1)} %param.4) | copy-start | bytes 786436
  391.1 25.0 %copy-start.1 = (f32[32,512]{1,0:T(8,128)S(1)}, f32[32,512]{1,0:T(8,128)}, u32[]{:S(2)}) copy-start(f32[32,512]{1,0:T(8,128)} %param.5) | copy-start | bytes 196612
  411.0 6.5 %collective-permute-start = (f32[128,1,512]{2,0,1:T(8,128)S(1)}, f32[128,1,512]{2,0,1:T(8,128)S(1)}, u32[]{:S(2)}, u32[]{:S(2)}) collective-permute-start(f32[128,1,512]{2,0,1:T(8,128)S(1)} %get-tuple-element.7), channel_id=1, source_target_pairs={{0,1},{1,2},{2,3},{3,4},{4,5},{5,6},{6,7},{7,8},{8,9},{9,10},{10,1... | collective-permute-start | bytes 786440 | tf_op jit(solution)/shard_map/ppermute | solution.py:14
  414.1 9.8 %collective-permute-start.1 = (f32[128,1,512]{2,0,1:T(8,128)S(1)}, f32[128,1,512]{2,0,1:T(8,128)S(1)}, u32[]{:S(2)}, u32[]{:S(2)}) collective-permute-start(f32[128,1,512]{2,0,1:T(8,128)S(1)} %get-tuple-element.8), channel_id=1, source_target_pairs={{1,0},{2,1},{3,2},{4,3},{5,4},{6,5},{7,6},{8,7},{9,8},{10,9},{11,1... | collective-permute-start | bytes 786440 | tf_op jit(solution)/shard_map/ppermute | solution.py:15
  443.9 5.2 %collective-permute-start.2 = (f32[128,1,512]{2,0,1:T(8,128)S(1)}, f32[128,1,512]{2,0,1:T(8,128)S(1)}, u32[]{:S(2)}, u32[]{:S(2)}) collective-permute-start(f32[128,1,512]{2,0,1:T(8,128)S(1)} %get-tuple-element.5), channel_id=1, source_target_pairs={{0,1},{1,2},{2,3},{3,4},{4,5},{5,6},{6,7},{7,8},{8,9},{9,10},{10,1... | collective-permute-start | bytes 786440 | tf_op jit(solution)/shard_map/ppermute | solution.py:14
  445.9 9.8 %collective-permute-start.3 = (f32[128,1,512]{2,0,1:T(8,128)S(1)}, f32[128,1,512]{2,0,1:T(8,128)S(1)}, u32[]{:S(2)}, u32[]{:S(2)}) collective-permute-start(f32[128,1,512]{2,0,1:T(8,128)S(1)} %get-tuple-element.6), channel_id=1, source_target_pairs={{1,0},{2,1},{3,2},{4,3},{5,4},{6,5},{7,6},{8,7},{9,8},{10,9},{11,1... | collective-permute-start | bytes 786440 | tf_op jit(solution)/shard_map/ppermute | solution.py:15
Sparse Core Ops, SparseCore 0:
  9.7 336.1 all-gather.1
where the time goes:
time: 495 us; the launch traced here: 493 us
  waiting for transfers between devices  354 us (72%)
  local copies, waits for them, and re-layouts  58.9 us (12%)
  other arithmetic  37.9 us (8%)
  matrix products  18.8 us (4%)
  between operations  13.5 us (3%)
  starting transfers between devices  9.59 us (2%)
    all_gather x1, waiting for transfers between devices, body(): piece = lax.all_gather(field, 'epoch', axis=0, tiled=True)  339 us
    reshape x1, local copies, waits for them, and re-layouts, body(): piece.reshape(many, slab * width)  45.1 us
    sub x2, other arithmetic, stencil(): (kappa + 4.0) * center  37.9 us
    dot_general x1, matrix products, body(): jnp.dot(lower, piece.reshape(many, slab * width), preferred_element_type=...  18.8 us
    ppermute x2, waiting for transfers between devices, with_halo(): after = lax.ppermute(first, axis, down)  13 us
    sub x1, local copies, waits for them, and re-layouts, stencil(): (kappa + 4.0) * center  11.6 us
  transfers between devices with their start and end apart: 5, of which 5 were waited for; matrix products, arithmetic and copies ran while one was open for 0% of the time, Pallas kernels for 0%

commit v1 on v0

--- a/solution.py
+++ b/solution.py
@@ -40,7 +40,9 @@
     )
     global_cols = lax.broadcasted_iota(jnp.int32, (epochs, order), 1)
     lower = jnp.where(global_cols <= global_rows, factor, jnp.zeros_like(factor))
-    piece = lax.all_gather(field, "epoch", axis=0, tiled=True)
+    piece = jnp.concatenate(
+        lax.all_to_all(jnp.stack([field] * lax.axis_size("epoch")), "epoch", 0, 0), axis=0
+    )
     many = piece.shape[0]
     timed = jnp.dot(
         lower, piece.reshape(many, slab * width), preferred_element_type=jnp.float32

time: 495 us -> 612 us (1.24)
  local copies, waits for them, and re-layouts: 58.9 us -> 154 us
  waiting for transfers between devices: 354 us -> 381 us
  between operations: 13.5 us -> 0.07 us
  starting transfers between devices: 9.59 us -> 17.5 us
    all_to_all x0 -> x1, waiting for transfers between devices: none -> 366 us  [body(): lax.all_to_all(jnp.stack([field] * lax.axis_size('epoch')), 'epoch', 0, 0)]
    all_gather x1 -> x0, waiting for transfers between devices: 339 us -> none  [body(): piece = lax.all_gather(field, 'epoch', axis=0, tiled=True)]
    reshape x1 -> x0, local copies, waits for them, and re-layouts: 45.1 us -> none  [body(): piece.reshape(many, slab * width)]
    all_to_all x0 -> x1, local copies, waits for them, and re-layouts: none -> 45 us  [body(): lax.all_to_all(jnp.stack([field] * lax.axis_size('epoch')), 'epoch', 0, 0)]
    dot_general x0 -> x1, local copies, waits for them, and re-layouts: none -> 44.1 us  [body(): jnp.dot(lower, piece.reshape(many, slab * width), preferred_element_type=...]
    unnamed x4 -> x6, local copies, waits for them, and re-layouts: 0.01 us -> 38.8 us
    another operation x0 -> x1, local copies, waits for them, and re-layouts: none -> 12.6 us  [body(): jnp.stack([field] * lax.axis_size('epoch'))]
    all_to_all x0 -> x1, starting transfers between devices: none -> 7.66 us  [body(): lax.all_to_all(jnp.stack([field] * lax.axis_size('epoch')), 'epoch', 0, 0)]
where the time goes in v1:
time: 612 us; the launch traced here: 609 us
  waiting for transfers between devices  381 us (62%)
  local copies, waits for them, and re-layouts  154 us (25%)
  other arithmetic  37.7 us (6%)
  matrix products  18.8 us (3%)
  starting transfers between devices  17.5 us (3%)
    all_to_all x1, waiting for transfers between devices, body(): lax.all_to_all(jnp.stack([field] * lax.axis_size('epoch')), 'epoch', 0, 0)  366 us
    all_to_all x1, local copies, waits for them, and re-layouts, body(): lax.all_to_all(jnp.stack([field] * lax.axis_size('epoch')), 'epoch', 0, 0)  45 us
    dot_general x1, local copies, waits for them, and re-layouts, body(): jnp.dot(lower, piece.reshape(many, slab * width), preferred_element_type=...  44.1 us
    unnamed x6, local copies, waits for them, and re-layouts  38.8 us
    sub x2, other arithmetic, stencil(): (kappa + 4.0) * center  37.7 us
    dot_general x1, matrix products, body(): jnp.dot(lower, piece.reshape(many, slab * width), preferred_element_type=...  18.8 us
    ppermute x2, waiting for transfers between devices, with_halo(): after = lax.ppermute(first, axis, down)  13 us
    another operation x1, local copies, waits for them, and re-layouts, body(): jnp.stack([field] * lax.axis_size('epoch'))  12.6 us
  transfers between devices with their start and end apart: 5, of which 5 were waited for; matrix products, arithmetic and copies ran while one was open for 0% of the time, Pallas kernels for 0%

profile of v1, /device:TPU:7, one launch (start us, length us, event | category | flops | bytes accessed | tf_op | source)
XLA Modules:
  0.0 609.4 jit_solution(6287054470292029109)
XLA Ops:
  0.0 7.9 %copy.8 = bf16[128,32,512]{0,2,1:T(8,128)(2,1)} copy(bf16[128,32,512]{2,1,0:T(8,128)(2,1)} %param.3) | data formatting | bytes 8388608 | tf_op args[0]
  7.9 12.6 %stack.2 = bf16[8,128,32,512]{1,3,2,0:T(8,128)(2,1)} broadcast(bf16[128,32,512]{0,2,1:T(8,128)(2,1)} %copy.8), dimensions={1,2,3} | broadcast | bytes 37748736 | tf_op jit(solution)/shard_map/stack | solution.py:44
  20.4 7.7 %all-to-all-start = ((bf16[8,128,32,512]{1,3,2,0:T(8,128)(2,1)}), bf16[8,128,32,512]{1,3,2,0:T(8,128)(2,1)}, u32[]{:S(2)}, u32[]{:S(2)}) async-start(bf16[8,128,32,512]{1,3,2,0:T(8,128)(2,1)} %stack.2), calls=%async_computation | async-start | bytes 67108864 | tf_op jit(solution)/shard_map/all_to_all | solution.py:44
  28.1 366.1 %all-to-all-done = bf16[8,128,32,512]{1,3,2,0:T(8,128)(2,1)} async-done(((bf16[8,128,32,512]{1,3,2,0:T(8,128)(2,1)}), bf16[8,128,32,512]{1,3,2,0:T(8,128)(2,1)}, u32[]{:S(2)}, u32[]{:S(2)}) %all-to-all-start) | async-done | bytes 33554464 | tf_op jit(solution)/shard_map/all_to_all | solution.py:44
  394.2 45.0 %copy.9 = bf16[8,128,32,512]{3,2,1,0:T(8,128)(2,1)} copy(bf16[8,128,32,512]{1,3,2,0:T(8,128)(2,1)} %all-to-all-done) | data formatting | bytes 67108864 | tf_op jit(solution)/shard_map/all_to_all | solution.py:44
  439.2 30.9 %copy.12 = bf16[128,8,32,512]{3,1,2,0:T(8,128)(2,1)} copy(bf16[128,8,32,512]{3,2,1,0:T(8,128)(2,1)} %bitcast.11) | data formatting | bytes 67108864
  470.1 0.0 copy-start
  470.1 44.1 %copy.10 = bf16[16384,1024]{1,0:T(8,128)(2,1)} copy(bf16[16384,1024]{0,1:T(8,128)(2,1)} %bitcast.12) | data formatting | bytes 67108864 | tf_op jit(solution)/shard_map/dot_general | solution.py:47
  514.2 0.0 copy-done
  514.2 0.0 copy-start.1
  514.2 18.8 %fusion.10 = f32[128,32,512]{2,0,1:T(8,128)} fusion(bf16[32,512,1024]{2,1,0:T(8,128)(2,1)} %bitcast.10, bf16[128,1024]{1,0:T(8,128)(2,1)S(1)} %copy-done, s32[128]{0:T(128)S(1)} %iota_add_fusion), kind=kOutput, calls=%fused_computation.19 | convolution fusion | flops 4295229440 | bytes 42205696 | tf_op jit(solution)/shard_map/dot_general | solution.py:47
  533.1 1.1 fusion.16
  534.1 3.4 collective-permute-start
  537.5 1.9 collective-permute-start.1
  539.4 0.0 copy-done.1
  539.4 1.3 collective-permute-done
  540.8 6.5 %collective-permute-done.1 = f32[128,1,512]{2,0,1:T(8,128)S(1)} collective-permute-done((f32[128,1,512]{2,0,1:T(8,128)S(1)}, f32[128,1,512]{2,0,1:T(8,128)S(1)}, u32[]{:S(2)}, u32[]{:S(2)}) %collective-permute-start.1) | collective-permute-done | bytes 262176 | tf_op jit(solution)/shard_map/ppermute | solution.py:15
  547.3 18.8 %fusion.2 = f32[128,32,512]{2,0,1:T(8,128)} fusion(f32[128,32,512]{2,0,1:T(8,128)} %fusion.10, f32[128,1,512]{2,0,1:T(8,128)S(1)} %collective-permute-done.1, f32[128,1,512]{2,0,1:T(8,128)S(1)} %collective-permute-done, f32[32,512]{1,0:T(8,128)S(1)} %broadcast_add_fusion), kind=kLoop, calls=%fused_computation.6 | loop fusion | flops 14680064 | bytes 17367040 | tf_op jit(solution)/shard_map/sub | solution.py:25
  566.1 1.1 fusion.15
  567.2 1.9 collective-permute-start.2
  569.1 2.6 collective-permute-start.3
  571.7 0.7 collective-permute-done.2
  572.4 6.5 %collective-permute-done.3 = f32[128,1,512]{2,0,1:T(8,128)S(1)} collective-permute-done((f32[128,1,512]{2,0,1:T(8,128)S(1)}, f32[128,1,512]{2,0,1:T(8,128)S(1)}, u32[]{:S(2)}, u32[]{:S(2)}) %collective-permute-start.3) | collective-permute-done | bytes 262176 | tf_op jit(solution)/shard_map/ppermute | solution.py:15
  578.9 18.9 %fusion.5 = f32[128,32,512]{2,0,1:T(8,128)} fusion(f32[128,32,512]{2,0,1:T(8,128)} %fusion.2, f32[128,1,512]{2,0,1:T(8,128)S(1)} %collective-permute-done.3, f32[128,1,512]{2,0,1:T(8,128)S(1)} %collective-permute-done.2, f32[32,512]{1,0:T(8,128)S(1)} %broadcast_add_fusion), kind=kLoop, calls=%fused_computation.9 | loop fusion | flops 14680064 | bytes 17367040 | tf_op jit(solution)/shard_map/sub | solution.py:25
  597.8 11.6 %copy.11 = f32[128,32,512]{2,1,0:T(8,128)} copy(f32[128,32,512]{2,0,1:T(8,128)} %fusion.5) | data formatting | bytes 16777216 | tf_op jit(solution)/shard_map/sub | solution.py:25
  (2 shorter events, 0.0 us)
Async XLA Ops:
  20.4 373.8 %all-to-all-start = ((bf16[8,128,32,512]{1,3,2,0:T(8,128)(2,1)}), bf16[8,128,32,512]{1,3,2,0:T(8,128)(2,1)}, u32[]{:S(2)}, u32[]{:S(2)}) async-start(bf16[8,128,32,512]{1,3,2,0:T(8,128)(2,1)} %stack.2), calls=%async_computation | async-start | bytes 67108864 | tf_op jit(solution)/shard_map/all_to_all | solution.py:44
  470.1 44.1 %copy-start = (bf16[128,1024]{1,0:T(8,128)(2,1)S(1)}, bf16[128,1024]{1,0:T(8,128)(2,1)}, u32[]{:S(2)}) copy-start(bf16[128,1024]{1,0:T(8,128)(2,1)} %param.4) | copy-start | bytes 786436
  514.2 25.2 %copy-start.1 = (f32[32,512]{1,0:T(8,128)S(1)}, f32[32,512]{1,0:T(8,128)}, u32[]{:S(2)}) copy-start(f32[32,512]{1,0:T(8,128)} %param.5) | copy-start | bytes 196612
  534.1 6.7 %collective-permute-start = (f32[128,1,512]{2,0,1:T(8,128)S(1)}, f32[128,1,512]{2,0,1:T(8,128)S(1)}, u32[]{:S(2)}, u32[]{:S(2)}) collective-permute-start(f32[128,1,512]{2,0,1:T(8,128)S(1)} %get-tuple-element.7), channel_id=1, source_target_pairs={{0,1},{1,2},{2,3},{3,4},{4,5},{5,6},{6,7},{7,8},{8,9},{9,10},{10,1... | collective-permute-start | bytes 786440 | tf_op jit(solution)/shard_map/ppermute | solution.py:14
  537.5 9.8 %collective-permute-start.1 = (f32[128,1,512]{2,0,1:T(8,128)S(1)}, f32[128,1,512]{2,0,1:T(8,128)S(1)}, u32[]{:S(2)}, u32[]{:S(2)}) collective-permute-start(f32[128,1,512]{2,0,1:T(8,128)S(1)} %get-tuple-element.8), channel_id=1, source_target_pairs={{1,0},{2,1},{3,2},{4,3},{5,4},{6,5},{7,6},{8,7},{9,8},{10,9},{11,1... | collective-permute-start | bytes 786440 | tf_op jit(solution)/shard_map/ppermute | solution.py:15
  567.2 5.2 collective-permute-start.2
  569.1 9.8 %collective-permute-start.3 = (f32[128,1,512]{2,0,1:T(8,128)S(1)}, f32[128,1,512]{2,0,1:T(8,128)S(1)}, u32[]{:S(2)}, u32[]{:S(2)}) collective-permute-start(f32[128,1,512]{2,0,1:T(8,128)S(1)} %get-tuple-element.6), channel_id=1, source_target_pairs={{1,0},{2,1},{3,2},{4,3},{5,4},{6,5},{7,6},{8,7},{9,8},{10,9},{11,1... | collective-permute-start | bytes 786440 | tf_op jit(solution)/shard_map/ppermute | solution.py:15
